TPU v7x, 512 devices: a whole 4x4x16 slice. The times are simulated.
512 devices in a mesh: expert: 8 (over y, core), mp: 64 (over x, z).
Axes of the slice: x: 4, y: 4, z: 16, core: 2. Of those that a mesh axis runs over, the one named last changes fastest.
Arguments:
- context: bfloat16 [4096, 2048], P('expert', 'mp'), may hold values from -6 to 6
- out_proj: bfloat16 [2048, 2048], P('mp'), may hold values from -1 to 1, as said below
- routes: int32 [4096, 2], P('expert'), may hold values from 0 to 7, all different within a row; in each aligned block of 512 rows (0 to 511, 512 to 1023, ...) at most 256 rows name the same one
- router_logits: float32 [4096, 2], P('expert'), may hold values from -8 to 8
- w_gate: bfloat16 [45056, 2048], P('mp', 'expert'), may hold values from -0.125 to 0.125
- w_up: bfloat16 [45056, 2048], P('mp', 'expert'), may hold values from -0.125 to 0.125
- w_down: bfloat16 [45056, 2048], P('mp', 'expert'), may hold values from -0.078125 to 0.078125
- norm_gain: float32 [2048], P('mp'), may hold values from 0.25 to 1.75
- request_order: int32 [4096], P('expert'), may hold values from 0 to 4095, each once
Outputs:
- restored: bfloat16 [4096, 2048], P('expert', 'mp')
Inputs may be any that keep to these rules, and one draw needn't show every extreme that they name: `routes`: each row names 2 different experts. Within each aligned block of 512 rows no expert is named by more than 256 rows, and in some blocks one expert is named by exactly 256 rows. `request_order`: A permutation of the 4096 token rows. `out_proj`: entries of the order of one over the square root of 2048.
All inputs are finite; a program needn't handle non-finite values.
Results may differ from a plain program's by a relative error of at most 0.0056.
Values may be sent and summed in bfloat16 or wider, within the bound.
No kernel may reach another device: no remote copies, remote signals or barrier semaphores. Data moves between devices by JAX's collectives and lax.ppermute only.
A program may use at most 64 MiB of HBM per device.

v0:
```python
import jax
import jax.numpy as jnp
from jax import lax
from jax.sharding import Mesh, PartitionSpec as P

EXPERTS = 8
CAP = 256
epsilon = 1e-06


def slot_targets(routes, capacity, experts):
    flat_routes = routes.reshape(-1)
    onehot = (flat_routes[:, None] == jnp.arange(experts, dtype=jnp.int32)[None, :]).astype(
        jnp.int32
    )
    earlier = jnp.cumsum(onehot, axis=0) - onehot
    slot_index = jnp.sum(earlier * onehot, axis=1)
    return flat_routes * capacity + slot_index


def shards(
    context, out_proj, routes, router_logits, w_gate, w_up, w_down, norm_gain, request_order
):
    tok_rows = context.shape[0]
    feat_local = context.shape[1]
    model_width = out_proj.shape[1]
    mp_count = lax.axis_size(MP)
    copies = mp_count // EXPERTS
    capacity = CAP
    top_k = routes.shape[1]
    x_count = lax.axis_size("mx")
    x_at = lax.axis_index("mx")
    along_z = lax.all_gather(context, MZ, axis=1, tiled=True)
    z_width = along_z.shape[1]
    rows_x = lax.all_to_all(
        jnp.broadcast_to(out_proj[None], (x_count,) + out_proj.shape),
        "mx",
        split_axis=0,
        concat_axis=0,
        tiled=True,
    ).reshape(x_count * feat_local, model_width)
    rows_x = lax.dynamic_slice_in_dim(rows_x, x_at * z_width, z_width, axis=1)
    partial_attended = jnp.einsum("td,cd->tc", along_z, rows_x, preferred_element_type=jnp.float32)
    attended = jnp.sum(
        lax.all_to_all(
            partial_attended.reshape(tok_rows, x_count, feat_local),
            "mx",
            split_axis=1,
            concat_axis=1,
            tiled=True,
        ),
        axis=1,
    ).astype(jnp.bfloat16)
    destination = slot_targets(routes, capacity, EXPERTS)
    source_rows = jnp.repeat(jnp.arange(tok_rows, dtype=jnp.int32), top_k)
    slotted = (
        jnp.zeros((EXPERTS * capacity, feat_local), jnp.bfloat16)
        .at[destination]
        .set(attended[source_rows])
    )
    one_copy = lax.all_to_all(
        slotted.reshape(EXPERTS, capacity, feat_local),
        ("mx", "mzh"),
        split_axis=0,
        concat_axis=0,
        tiled=True,
    )
    inbox_rows = (
        lax.all_gather(one_copy, "mzl", axis=0)
        .transpose(2, 1, 0, 3)
        .reshape(capacity, mp_count * feat_local)
    )
    stacked = lax.all_gather(jnp.stack([w_gate, w_up, w_down]), EX, axis=2, tiled=True)
    gate_next = jnp.einsum("rd,hd->rh", inbox_rows, stacked[0], preferred_element_type=jnp.float32)
    up_next = jnp.einsum("rd,hd->rh", inbox_rows, stacked[1], preferred_element_type=jnp.float32)
    activated = (jax.nn.silu(gate_next) * up_next).astype(jnp.bfloat16)
    partial_value = jnp.dot(activated, stacked[2], preferred_element_type=jnp.float32)
    returned = lax.all_to_all(
        partial_value.astype(jnp.bfloat16), MP, split_axis=1, concat_axis=0, tiled=True
    )
    expert_out = jnp.sum(
        returned.reshape(EXPERTS, copies, capacity, feat_local).astype(jnp.float32), axis=1
    ).reshape(EXPERTS * capacity, feat_local)
    picked = expert_out[destination].reshape(tok_rows, top_k, feat_local)
    weights = 1.0 / (1.0 + jnp.exp(router_logits[:, ::-1] - router_logits))
    branch = jnp.sum(picked * weights[:, :, None], axis=1)
    combined = attended.astype(jnp.float32) + branch
    squares = jnp.sum(lax.all_gather(jnp.sum(combined * combined, axis=1), MZ, axis=0), axis=0)
    squares = jnp.sum(lax.all_gather(squares, "mx", axis=0), axis=0)
    normed = (
        combined * norm_gain[None, :] * lax.rsqrt(squares / model_width + epsilon)[:, None]
    ).astype(jnp.bfloat16)
    everyone = lax.all_gather(normed, EX, axis=0, tiled=True)
    return everyone[request_order]


EX = ("ey", "ec")
MZ = ("mzh", "mzl")
MP = ("mx",) + MZ


def split_mesh(mesh):
    devices = mesh.devices
    n_exp, n_mp = devices.shape
    row = devices[0].reshape(-1)
    try:
        z_count = len({d.coords[2] for d in row})
    except (AttributeError, IndexError, TypeError):
        z_count = n_mp
    group = n_mp // EXPERTS
    return Mesh(
        devices.reshape(1, n_exp, n_mp // z_count, z_count // group, group),
        ("ey", "ec", "mx", "mzh", "mzl"),
    )


def solution(mesh):
    fine = split_mesh(mesh)
    placed = (
        P(EX, MP),
        P(MP, None),
        P(EX, None),
        P(EX, None),
        P(MP, EX),
        P(MP, EX),
        P(MP, EX),
        P(MP),
        P(EX),
    )
    return jax.shard_map(shards, mesh=fine, in_specs=placed, out_specs=P(EX, MP), check_vma=False)
```

profile of v0, /device:TPU:1, one launch (start us, length us, event | category | flops | bytes accessed | tf_op | source)
XLA Modules:
  0.0 365.1 jit_solution(336323215488150138)
XLA Ops:
  6.5 1.7 broadcast_in_dim.8
  8.3 4.8 %all-to-all-start = ((bf16[4,32,2048]{2,1,0:T(8,128)(2,1)}), bf16[4,32,2048]{2,1,0:T(8,128)(2,1)S(1)}, u32[]{:S(2)}, u32[]{:S(2)}) async-start(bf16[4,32,2048]{2,1,0:T(8,128)(2,1)} %broadcast_in_dim.8), calls=%async_computation | async-start | bytes 1048576 | tf_op jit(solution)/shard_map/all_to_all | solution.py:35
  13.1 0.8 copy.77
  14.3 0.8 broadcast_multiply_fusion
  15.1 2.3 reduce-window.6
  17.4 0.3 slice_reduce_fusion
  18.1 0.2 mul.59
  18.5 31.9 %all_gather.27 = bf16[512,512]{0,1:T(8,128)(2,1)S(1)} all-gather(bf16[512,32]{0,1:T(8,128)(2,1)S(1)} %copy-done.3), channel_id=1, replica_groups=mesh['ey'=1,'ec'=8,'mx'=4,'mzh'=2,'mzl'=8] {'mzh','mzl'}, dimensions={1}, use_global_device_ids=true | all-gather | bytes 557056 | tf_op jit(solution)/shard_map/all_gather | solution.py:33
  50.5 0.9 fusion.15
  51.4 4.1 %all-to-all-start.1 = ((f32[512,4,32]{0,2,1:T(8,128)}), f32[512,4,32]{0,2,1:T(8,128)S(1)}, u32[]{:S(2)}, u32[]{:S(2)}) async-start(f32[512,4,32]{0,2,1:T(8,128)} %bitcast.2), calls=%async_computation.1 | async-start | bytes 524288 | tf_op jit(solution)/shard_map/all_to_all | solution.py:45
  55.5 5.5 %all-to-all-done.1 = f32[512,4,32]{0,2,1:T(8,128)S(1)} async-done(((f32[512,4,32]{0,2,1:T(8,128)}), f32[512,4,32]{0,2,1:T(8,128)S(1)}, u32[]{:S(2)}, u32[]{:S(2)}) %all-to-all-start.1) | async-done | bytes 262176 | tf_op jit(solution)/shard_map/all_to_all | solution.py:45
  61.1 6.4 %scatter_custom_fusion = bf16[2048,32]{1,0:T(8,128)(2,1)S(1)} fusion(s32[1024]{0:T(1024)S(1)} %bitcast.74, bf16[512,32]{1,0:T(8,128)(2,1)S(1)} %copy.79, s32[1024]{0:T(1024)S(1)} %broadcast_clamp_fusion.1, bf16[]{:T(256)} %constant.18.clone.1), kind=kCustom, calls=%fused_computation.22 | custom fusion | bytes 131074 | tf_op jit(solution)/shard_map/scatter | solution.py:59
  67.5 0.2 copy.81
  67.7 20.9 %all_to_all.28 = bf16[8,256,32]{1,2,0:T(8,128)(2,1)} all-to-all(bf16[8,256,32]{1,2,0:T(8,128)(2,1)S(1)} %copy.81), channel_id=1, replica_groups=mesh['ey'=1,'ec'=8,'mx'=4,'mzh'=2,'mzl'=8] {'mx','mzh'}, dimensions={0} | all-to-all | bytes 262144 | tf_op jit(solution)/shard_map/all_to_all | solution.py:61
  88.8 1.2 pad_maximum_fusion
  90.0 62.6 %all-gather.10.cloned.1.call-done = bf16[64,256,32]{1,2,0:T(8,128)(2,1)} async-done(((bf16[8,256,32]{1,2,0:T(8,128)(2,1)}), bf16[64,256,32]{1,2,0:T(8,128)(2,1)}) %all-gather.10.cloned.1.call-update) | async-done | bytes 1048592 | tf_op jit(solution)/shard_map/all_gather | solution.py:69
  152.6 1.3 copy.82
  153.9 64.0 %all-gather.8.cloned.1.call-done = bf16[3,704,2048]{2,1,0:T(8,128)(2,1)} async-done(((bf16[3,704,256]{2,1,0:T(8,128)(2,1)}), bf16[3,704,2048]{2,1,0:T(8,128)(2,1)}) %all-gather.8.cloned.1.call-update) | async-done | bytes 8650768 | tf_op jit(solution)/shard_map/all_gather | solution.py:73
  217.9 2.7 fusion.2
  220.6 6.0 %fusion.3 = bf16[256,2048]{1,0:T(8,128)(2,1)S(1)} fusion(bf16[3,704,2048]{2,1,0:T(8,128)(2,1)} %all-gather.8.cloned.1.call-done, bf16[256,2048]{0,1:T(8,128)(2,1)S(1)} %bitcast.68, f32[256,704]{0,1:T(8,128)S(1)} %fusion.2), kind=kOutput, calls=%fused_computation.10 | convolution fusion | flops 1478000640 | bytes 8585216 | tf_op jit(solution)/shard_map/dot_general | solution.py:77
  226.6 1.3 copy.83
  227.9 15.5 %all-to-all-start.3 = ((bf16[256,64,32]{0,2,1:T(8,128)(2,1)}), bf16[256,64,32]{0,2,1:T(8,128)(2,1)S(1)}, u32[]{:S(2)}, u32[]{:S(2)}) async-start(bf16[256,64,32]{0,2,1:T(8,128)(2,1)} %bitcast.17), calls=%async_computation.3 | async-start | bytes 2097152 | tf_op jit(solution)/shard_map/all_to_all | solution.py:78
  243.8 50.3 %all-to-all-done.3 = bf16[256,64,32]{0,2,1:T(8,128)(2,1)S(1)} async-done(((bf16[256,64,32]{0,2,1:T(8,128)(2,1)}), bf16[256,64,32]{0,2,1:T(8,128)(2,1)S(1)}, u32[]{:S(2)}, u32[]{:S(2)}) %all-to-all-start.3) | async-done | bytes 1048608 | tf_op jit(solution)/shard_map/all_to_all | solution.py:78
  294.3 0.3 copy.84
  294.6 2.8 gather_fusion
  297.4 2.8 multiply_reduce_fusion
  300.4 22.4 %all-gather.3 = f32[16,1,512]{2,1,0:T(1,128)S(1)} all-gather(f32[1,1,512]{2,1,0:T(1,128)S(1)} %bitcast.79), channel_id=3, replica_groups=mesh['ey'=1,'ec'=8,'mx'=4,'mzh'=2,'mzl'=8] {'mzh','mzl'}, dimensions={0}, use_global_device_ids=true | all-gather | bytes 34816 | tf_op jit(solution)/shard_map/all_gather | solution.py:88
  322.8 9.5 %all-gather.4 = f32[4,1,512]{2,1,0:T(1,128)S(1)} all-gather(f32[1,1,512]{2,1,0:T(1,128)S(1)} %bitcast.78), channel_id=4, replica_groups=mesh['ey'=1,'ec'=8,'mx'=4,'mzh'=2,'mzl'=8] {'mx'}, dimensions={0}, use_global_device_ids=true | all-gather | bytes 10240 | tf_op jit(solution)/shard_map/all_gather | solution.py:89
  332.5 23.2 %all_gather.35 = bf16[4096,32]{0,1:T(8,128)(2,1)S(1)} all-gather(bf16[512,32]{0,1:T(8,128)(2,1)S(1)} %multiply_convert_fusion), channel_id=1, replica_groups=mesh['ey'=1,'ec'=8,'mx'=4,'mzh'=2,'mzl'=8] {'ey','ec'}, dimensions={0}, use_global_device_ids=true | all-gather | bytes 294912 | tf_op jit(solution)/shard_map/all_gather | solution.py:93
  355.8 0.5 copy.87
  356.2 1.3 gather_fusion.1
  357.6 0.7 copy.88
  (46 shorter events, 2.0 us)
Async XLA Ops:
  6.5 12.0 %copy-start.3 = (bf16[512,32]{0,1:T(8,128)(2,1)S(1)}, bf16[512,32]{0,1:T(8,128)(2,1)}, u32[]{:S(2)}) copy-start(bf16[512,32]{0,1:T(8,128)(2,1)} %param.9) | copy-start | bytes 98308
  8.3 42.2 %all-to-all-start = ((bf16[4,32,2048]{2,1,0:T(8,128)(2,1)}), bf16[4,32,2048]{2,1,0:T(8,128)(2,1)S(1)}, u32[]{:S(2)}, u32[]{:S(2)}) async-start(bf16[4,32,2048]{2,1,0:T(8,128)(2,1)} %broadcast_in_dim.8), calls=%async_computation | async-start | bytes 1048576 | tf_op jit(solution)/shard_map/all_to_all | solution.py:35
  14.1 74.6 %copy-start = (bf16[704,256]{1,0:T(8,128)(2,1)S(1)}, bf16[704,256]{1,0:T(8,128)(2,1)}, u32[]{:S(2)}) copy-start(bf16[704,256]{1,0:T(8,128)(2,1)} %param.15) | copy-start | bytes 1081348
  14.1 74.6 %copy-start.1 = (bf16[704,256]{1,0:T(8,128)(2,1)S(1)}, bf16[704,256]{1,0:T(8,128)(2,1)}, u32[]{:S(2)}) copy-start(bf16[704,256]{1,0:T(8,128)(2,1)} %param.14) | copy-start | bytes 1081348
  14.2 74.6 %copy-start.2 = (bf16[704,256]{1,0:T(8,128)(2,1)S(1)}, bf16[704,256]{1,0:T(8,128)(2,1)}, u32[]{:S(2)}) copy-start(bf16[704,256]{1,0:T(8,128)(2,1)} %param.13) | copy-start | bytes 1081348
  51.4 9.6 %all-to-all-start.1 = ((f32[512,4,32]{0,2,1:T(8,128)}), f32[512,4,32]{0,2,1:T(8,128)S(1)}, u32[]{:S(2)}, u32[]{:S(2)}) async-start(f32[512,4,32]{0,2,1:T(8,128)} %bitcast.2), calls=%async_computation.1 | async-start | bytes 524288 | tf_op jit(solution)/shard_map/all_to_all | solution.py:45
  55.4 97.1 %all-gather.10.cloned.1.call-start = ((), (), s32[]{:S(2)}) async-start(), calls=%async_computation.5 | async-start | bytes 1179648 | tf_op jit(solution)/shard_map/all_gather | solution.py:69
  88.7 129.2 %all-gather.8.cloned.1.call-start = ((), (), s32[]{:S(2)}) async-start(), calls=%async_computation.4 | async-start | bytes 9732096 | tf_op jit(solution)/shard_map/all_gather | solution.py:73
  226.6 16.9 %copy-start.4 = (f32[512,2]{0,1:T(2,128)S(1)}, f32[512,2]{0,1:T(2,128)}, u32[]{:S(2)}) copy-start(f32[512,2]{0,1:T(2,128)} %param.12) | copy-start | bytes 12292
  226.6 17.2 %copy-start.5 = (s32[512]{0:T(512)S(1)}, s32[512]{0:T(512)}, u32[]{:S(2)}) copy-start(s32[512]{0:T(512)} %param.17) | copy-start | bytes 6148
  227.9 66.2 %all-to-all-start.3 = ((bf16[256,64,32]{0,2,1:T(8,128)(2,1)}), bf16[256,64,32]{0,2,1:T(8,128)(2,1)S(1)}, u32[]{:S(2)}, u32[]{:S(2)}) async-start(bf16[256,64,32]{0,2,1:T(8,128)(2,1)} %bitcast.17), calls=%async_computation.3 | async-start | bytes 2097152 | tf_op jit(solution)/shard_map/all_to_all | solution.py:78
  294.6 37.8 %copy-start.6 = (f32[32]{0:T(128)S(1)}, f32[32]{0:T(128)}, u32[]{:S(2)}) copy-start(f32[32]{0:T(128)} %param.16) | copy-start | bytes 388
Sparse Core Ops, SparseCore 0:
  88.8 63.6 all-gather.9
  154.7 63.1 all-gather.7
where the time goes:
time: 366 us; the launch traced here: 365 us
  waiting for transfers between devices  182 us (50%)
  blocking collectives  108 us (30%)
  starting transfers between devices  24.5 us (7%)
  local copies, waits for them, and re-layouts  19.2 us (5%)
  between operations  13.7 us (4%)
  matrix products  9.63 us (3%)
  other arithmetic  7.73 us (2%)
    all_gather x1, waiting for transfers between devices, shards(): lax.all_gather(jnp.stack([w_gate, w_up, w_down]), EX, axis=2, tiled=True)  64 us
    all_gather x1, waiting for transfers between devices, shards(): lax.all_gather(one_copy, 'mzl', axis=0).transpose(2, 1, 0, 3)  62.6 us
    all_to_all x1, waiting for transfers between devices, shards(): lax.all_to_all(partial_value.astype(jnp.bfloat16), MP, split_axis=1, conc...  50.3 us
    all_gather x1, blocking collectives, shards(): along_z = lax.all_gather(context, MZ, axis=1, tiled=True)  31.9 us
    all_gather x1, blocking collectives, shards(): everyone = lax.all_gather(normed, EX, axis=0, tiled=True)  23.2 us
    all_gather x1, blocking collectives, shards(): lax.all_gather(jnp.sum(combined * combined, axis=1), MZ, axis=0)  22.4 us
    all_to_all x1, blocking collectives, shards(): lax.all_to_all(slotted.reshape(EXPERTS, capacity, feat_local), ('mx', 'mz...  20.9 us
    all_to_all x1, starting transfers between devices, shards(): lax.all_to_all(partial_value.astype(jnp.bfloat16), MP, split_axis=1, conc...  15.5 us
  transfers between devices with their start and end apart: 5, of which 4 were waited for; matrix products, arithmetic and copies ran while one was open for 2% of the time, Pallas kernels for 0%

commit v1 on v0

--- a/solution.py
+++ b/solution.py
@@ -70,7 +70,11 @@
         .transpose(2, 1, 0, 3)
         .reshape(capacity, mp_count * feat_local)
     )
-    stacked = lax.all_gather(jnp.stack([w_gate, w_up, w_down]), EX, axis=2, tiled=True)
+    part = jnp.stack([w_gate, w_up, w_down])
+    count = lax.axis_size(EX)
+    blocks = jnp.stack([part for _ in range(count)])
+    blocks = lax.all_to_all(blocks, EX, split_axis=0, concat_axis=0)
+    stacked = jnp.concatenate(blocks, axis=2)
     gate_next = jnp.einsum("rd,hd->rh", inbox_rows, stacked[0], preferred_element_type=jnp.float32)
     up_next = jnp.einsum("rd,hd->rh", inbox_rows, stacked[1], preferred_element_type=jnp.float32)
     activated = (jax.nn.silu(gate_next) * up_next).astype(jnp.bfloat16)

time: 366 us -> 353 us (0.964)
  blocking collectives: 108 us -> 87.2 us
  waiting for transfers between devices: 182 us -> 164 us
  local copies, waits for them, and re-layouts: 19.2 us -> 33.6 us
  starting transfers between devices: 24.5 us -> 37.9 us
    all_gather x1 -> x0, waiting for transfers between devices: 64 us -> none  [shards(): lax.all_gather(jnp.stack([w_gate, w_up, w_down]), EX, axis=2, tiled=True)]
    all_to_all x0 -> x2, waiting for transfers between devices: none -> 52.7 us  [the longest x1 38.6 us: shards(): blocks = lax.all_to_all(blocks, EX, split_axis=0, concat_axis=0)]
    all_to_all x0 -> x2, starting transfers between devices: none -> 22.8 us  [the longest x1 16 us: shards(): blocks = lax.all_to_all(blocks, EX, split_axis=0, concat_axis=0)]
    all_to_all x1 -> x0, blocking collectives: 20.9 us -> none  [shards(): lax.all_to_all(slotted.reshape(EXPERTS, capacity, feat_local), ('mx', 'mz...]
    all_to_all x1, starting transfers between devices: 15.5 us -> 6.03 us  [shards(): lax.all_to_all(partial_value.astype(jnp.bfloat16), MP, split_axis=1, conc...]
    all_gather x1, waiting for transfers between devices: 62.6 us -> 55.1 us  [shards(): lax.all_gather(one_copy, 'mzl', axis=0).transpose(2, 1, 0, 3)]
    another operation x0 -> x1, local copies, waits for them, and re-layouts: none -> 4.24 us  [shards(): blocks = jnp.stack([part for _ in range(count)])]
    slice x1 -> x2, local copies, waits for them, and re-layouts: 0.28 us -> 4.29 us  [the longest x1 4.01 us: shards(): stacked[0]]
  transfers between devices with their start and end apart: 5 -> 6, of which waited for: 4 -> 5; matrix products, arithmetic and copies ran while one was open for 2% -> 2% of each run, Pallas kernels for 0% -> 0%
where the time goes in v1:
time: 353 us; the launch traced here: 352 us
  waiting for transfers between devices  164 us (46%)
  blocking collectives  87.2 us (25%)
  starting transfers between devices  37.9 us (11%)
  local copies, waits for them, and re-layouts  33.6 us (10%)
  between operations  13.7 us (4%)
  matrix products  9.22 us (3%)
  other arithmetic  6.57 us (2%)
    all_gather x1, waiting for transfers between devices, shards(): lax.all_gather(one_copy, 'mzl', axis=0).transpose(2, 1, 0, 3)  55.1 us
    all_to_all x1, waiting for transfers between devices, shards(): lax.all_to_all(partial_value.astype(jnp.bfloat16), MP, split_axis=1, conc...  49.9 us
    all_to_all x1, waiting for transfers between devices, shards(): blocks = lax.all_to_all(blocks, EX, split_axis=0, concat_axis=0)  38.6 us
    all_gather x1, blocking collectives, shards(): along_z = lax.all_gather(context, MZ, axis=1, tiled=True)  31.7 us
    all_gather x1, blocking collectives, shards(): everyone = lax.all_gather(normed, EX, axis=0, tiled=True)  24.6 us
    all_gather x1, blocking collectives, shards(): lax.all_gather(jnp.sum(combined * combined, axis=1), MZ, axis=0)  22.5 us
    all_to_all x1, starting transfers between devices, shards(): blocks = lax.all_to_all(blocks, EX, split_axis=0, concat_axis=0)  16 us
    all_to_all x1, waiting for transfers between devices, shards(): lax.all_to_all(slotted.reshape(EXPERTS, capacity, feat_local), ('mx', 'mz...  14.1 us
  transfers between devices with their start and end apart: 6, of which 5 were waited for; matrix products, arithmetic and copies ran while one was open for 2% of the time, Pallas kernels for 0%

profile of v1, /device:TPU:1, one launch (start us, length us, event | category | flops | bytes accessed | tf_op | source)
XLA Modules:
  0.0 352.0 jit_solution(13428595350731919591)
XLA Ops:
  6.5 1.7 broadcast_in_dim.8
  8.3 4.8 %all-to-all-start = ((bf16[4,32,2048]{2,1,0:T(8,128)(2,1)}), bf16[4,32,2048]{2,1,0:T(8,128)(2,1)S(1)}, u32[]{:S(2)}, u32[]{:S(2)}) async-start(bf16[4,32,2048]{2,1,0:T(8,128)(2,1)} %broadcast_in_dim.8), calls=%async_computation | async-start | bytes 1048576 | tf_op jit(solution)/shard_map/all_to_all | solution.py:35
  13.8 0.8 copy.86
  15.4 2.3 reduce-window.6
  18.4 31.7 %all_gather.24 = bf16[512,512]{0,1:T(8,128)(2,1)S(1)} all-gather(bf16[512,32]{0,1:T(8,128)(2,1)S(1)} %copy-done.5), channel_id=1, replica_groups=mesh['ey'=1,'ec'=8,'mx'=4,'mzh'=2,'mzl'=8] {'mzh','mzl'}, dimensions={1}, use_global_device_ids=true | all-gather | bytes 557056 | tf_op jit(solution)/shard_map/all_gather | solution.py:33
  50.2 0.9 fusion.5
  51.1 4.2 %all-to-all-start.1 = ((f32[512,4,32]{0,2,1:T(8,128)}), f32[512,4,32]{0,2,1:T(8,128)S(1)}, u32[]{:S(2)}, u32[]{:S(2)}) async-start(f32[512,4,32]{0,2,1:T(8,128)} %bitcast.2), calls=%async_computation.1 | async-start | bytes 524288 | tf_op jit(solution)/shard_map/all_to_all | solution.py:45
  55.4 5.5 %all-to-all-done.1 = f32[512,4,32]{0,2,1:T(8,128)S(1)} async-done(((f32[512,4,32]{0,2,1:T(8,128)}), f32[512,4,32]{0,2,1:T(8,128)S(1)}, u32[]{:S(2)}, u32[]{:S(2)}) %all-to-all-start.1) | async-done | bytes 262176 | tf_op jit(solution)/shard_map/all_to_all | solution.py:45
  61.0 6.4 %scatter_custom_fusion = bf16[2048,32]{1,0:T(8,128)(2,1)S(1)} fusion(s32[1024]{0:T(1024)S(1)} %bitcast.79, bf16[512,32]{1,0:T(8,128)(2,1)S(1)} %copy.88, s32[1024]{0:T(1024)S(1)} %broadcast_clamp_fusion.1, bf16[]{:T(256)} %constant.18.clone.1), kind=kCustom, calls=%fused_computation.11 | custom fusion | bytes 131074 | tf_op jit(solution)/shard_map/scatter | solution.py:59
  67.4 0.8 copy.90
  68.3 6.8 %all-to-all-start.2 = ((bf16[8,256,32]{1,2,0:T(8,128)(2,1)}), bf16[8,256,32]{1,2,0:T(8,128)(2,1)S(1)}, u32[]{:S(2)}, u32[]{:S(2)}) async-start(bf16[8,256,32]{1,2,0:T(8,128)(2,1)} %copy.90), calls=%async_computation.2 | async-start | bytes 262144 | tf_op jit(solution)/shard_map/all_to_all | solution.py:61
  75.2 14.1 %all-to-all-done.2 = bf16[8,256,32]{1,2,0:T(8,128)(2,1)S(1)} async-done(((bf16[8,256,32]{1,2,0:T(8,128)(2,1)}), bf16[8,256,32]{1,2,0:T(8,128)(2,1)S(1)}, u32[]{:S(2)}, u32[]{:S(2)}) %all-to-all-start.2) | async-done | bytes 131104 | tf_op jit(solution)/shard_map/all_to_all | solution.py:61
  89.3 4.2 %stack.27 = bf16[8,3,704,256]{3,2,1,0:T(8,128)(2,1)} broadcast(bf16[3,704,256]{2,1,0:T(8,128)(2,1)S(1)} %pad_maximum_fusion), dimensions={1,2,3} | broadcast | bytes 9732096 | tf_op jit(solution)/shard_map/stack | solution.py:75
  93.6 16.0 %all-to-all-start.3 = ((bf16[8,3,704,256]{3,2,1,0:T(8,128)(2,1)}), bf16[8,3,704,256]{3,2,1,0:T(8,128)(2,1)}, u32[]{:S(2)}, u32[]{:S(2)}) async-start(bf16[8,3,704,256]{3,2,1,0:T(8,128)(2,1)} %stack.27), calls=%async_computation.3 | async-start | bytes 17301504 | tf_op jit(solution)/shard_map/all_to_all | solution.py:76
  109.6 0.7 all-gather.7.cloned.1.call-update
  110.3 55.1 %all-gather.7.cloned.1.call-done = bf16[64,256,32]{1,2,0:T(8,128)(2,1)} async-done(((bf16[8,256,32]{1,2,0:T(8,128)(2,1)}), bf16[64,256,32]{1,2,0:T(8,128)(2,1)}) %all-gather.7.cloned.1.call-update) | async-done | bytes 1048592 | tf_op jit(solution)/shard_map/all_gather | solution.py:69
  165.4 2.3 copy.91
  167.7 38.6 %all-to-all-done.3 = bf16[8,3,704,256]{3,2,1,0:T(8,128)(2,1)} async-done(((bf16[8,3,704,256]{3,2,1,0:T(8,128)(2,1)}), bf16[8,3,704,256]{3,2,1,0:T(8,128)(2,1)}, u32[]{:S(2)}, u32[]{:S(2)}) %all-to-all-start.3) | async-done | bytes 8650784 | tf_op jit(solution)/shard_map/all_to_all | solution.py:76
  206.3 4.0 %fusion.13 = (bf16[1,704,8,256]{3,1,0,2:T(8,128)(2,1)S(1)}, bf16[1,704,8,256]{3,1,0,2:T(8,128)(2,1)S(1)}, bf16[1,704,8,256]{3,1,0,2:T(8,128)(2,1)S(1)}) fusion(bf16[3,704,8,256]{3,1,0,2:T(8,128)(2,1)} %bitcast.14), kind=kLoop, calls=%fused_computation.39 | loop fusion | bytes 17301504 | tf_op jit(solution)/shard_map/slice | solution.py:78
  210.7 2.0 copy.105
  213.0 0.8 copy-done
  213.9 1.8 fusion.14
  215.7 6.5 %convolution_convert_fusion = bf16[256,2048]{1,0:T(8,128)(2,1)} fusion(bf16[704,2048]{1,0:T(8,128)(2,1)S(1)} %bitcast.66, bf16[704,2048]{1,0:T(8,128)(2,1)} %bitcast.67, bf16[256,2048]{0,1:T(8,128)(2,1)} %bitcast.71, f32[256,704]{0,1:T(8,128)} %fusion.14), kind=kOutput, calls=%fused_computation.4 | convolution fusion | flops 1478000640 | bytes 8585216 | tf_op jit(solution)/shard_map/dot_general | solution.py:81
  222.2 2.3 copy.95
  224.5 6.0 %all-to-all-start.4 = ((bf16[256,64,32]{0,2,1:T(8,128)(2,1)}), bf16[256,64,32]{0,2,1:T(8,128)(2,1)S(1)}, u32[]{:S(2)}, u32[]{:S(2)}) async-start(bf16[256,64,32]{0,2,1:T(8,128)(2,1)} %bitcast.15), calls=%async_computation.4 | async-start | bytes 2097152 | tf_op jit(solution)/shard_map/all_to_all | solution.py:82
  230.9 49.9 %all-to-all-done.4 = bf16[256,64,32]{0,2,1:T(8,128)(2,1)S(1)} async-done(((bf16[256,64,32]{0,2,1:T(8,128)(2,1)}), bf16[256,64,32]{0,2,1:T(8,128)(2,1)S(1)}, u32[]{:S(2)}, u32[]{:S(2)}) %all-to-all-start.4) | async-done | bytes 1048608 | tf_op jit(solution)/shard_map/all_to_all | solution.py:82
  281.3 2.8 gather_fusion
  284.1 2.8 multiply_reduce_fusion
  287.0 22.5 %all-gather.3 = f32[16,1,512]{2,1,0:T(1,128)S(1)} all-gather(f32[1,1,512]{2,1,0:T(1,128)S(1)} %bitcast.84), channel_id=3, replica_groups=mesh['ey'=1,'ec'=8,'mx'=4,'mzh'=2,'mzl'=8] {'mzh','mzl'}, dimensions={0}, use_global_device_ids=true | all-gather | bytes 34816 | tf_op jit(solution)/shard_map/all_gather | solution.py:92
  309.6 8.4 %all-gather.4 = f32[4,1,512]{2,1,0:T(1,128)S(1)} all-gather(f32[1,1,512]{2,1,0:T(1,128)S(1)} %bitcast.83), channel_id=4, replica_groups=mesh['ey'=1,'ec'=8,'mx'=4,'mzh'=2,'mzl'=8] {'mx'}, dimensions={0}, use_global_device_ids=true | all-gather | bytes 10240 | tf_op jit(solution)/shard_map/all_gather | solution.py:93
  318.1 24.6 %all_gather.31 = bf16[4096,32]{0,1:T(8,128)(2,1)S(1)} all-gather(bf16[512,32]{0,1:T(8,128)(2,1)S(1)} %multiply_convert_fusion), channel_id=1, replica_groups=mesh['ey'=1,'ec'=8,'mx'=4,'mzh'=2,'mzl'=8] {'ey','ec'}, dimensions={0}, use_global_device_ids=true | all-gather | bytes 294912 | tf_op jit(solution)/shard_map/all_gather | solution.py:97
  343.1 1.3 gather_fusion.1
  (55 shorter events, 5.4 us)
Async XLA Ops:
  6.5 11.9 %copy-start.5 = (bf16[512,32]{0,1:T(8,128)(2,1)S(1)}, bf16[512,32]{0,1:T(8,128)(2,1)}, u32[]{:S(2)}) copy-start(bf16[512,32]{0,1:T(8,128)(2,1)} %param.9) | copy-start | bytes 98308
  8.3 41.9 %all-to-all-start = ((bf16[4,32,2048]{2,1,0:T(8,128)(2,1)}), bf16[4,32,2048]{2,1,0:T(8,128)(2,1)S(1)}, u32[]{:S(2)}, u32[]{:S(2)}) async-start(bf16[4,32,2048]{2,1,0:T(8,128)(2,1)} %broadcast_in_dim.8), calls=%async_computation | async-start | bytes 1048576 | tf_op jit(solution)/shard_map/all_to_all | solution.py:35
  14.7 60.4 %copy-start.2 = (bf16[704,256]{1,0:T(8,128)(2,1)S(1)}, bf16[704,256]{1,0:T(8,128)(2,1)}, u32[]{:S(2)}) copy-start(bf16[704,256]{1,0:T(8,128)(2,1)} %param.15) | copy-start | bytes 1081348
  14.7 60.4 %copy-start.3 = (bf16[704,256]{1,0:T(8,128)(2,1)S(1)}, bf16[704,256]{1,0:T(8,128)(2,1)}, u32[]{:S(2)}) copy-start(bf16[704,256]{1,0:T(8,128)(2,1)} %param.14) | copy-start | bytes 1081348
  14.7 60.4 %copy-start.4 = (bf16[704,256]{1,0:T(8,128)(2,1)S(1)}, bf16[704,256]{1,0:T(8,128)(2,1)}, u32[]{:S(2)}) copy-start(bf16[704,256]{1,0:T(8,128)(2,1)} %param.13) | copy-start | bytes 1081348
  51.1 9.8 %all-to-all-start.1 = ((f32[512,4,32]{0,2,1:T(8,128)}), f32[512,4,32]{0,2,1:T(8,128)S(1)}, u32[]{:S(2)}, u32[]{:S(2)}) async-start(f32[512,4,32]{0,2,1:T(8,128)} %bitcast.2), calls=%async_computation.1 | async-start | bytes 524288 | tf_op jit(solution)/shard_map/all_to_all | solution.py:45
  68.3 21.0 %all-to-all-start.2 = ((bf16[8,256,32]{1,2,0:T(8,128)(2,1)}), bf16[8,256,32]{1,2,0:T(8,128)(2,1)S(1)}, u32[]{:S(2)}, u32[]{:S(2)}) async-start(bf16[8,256,32]{1,2,0:T(8,128)(2,1)} %copy.90), calls=%async_computation.2 | async-start | bytes 262144 | tf_op jit(solution)/shard_map/all_to_all | solution.py:61
  89.3 4.2 %copy-start.1 = (bf16[8,256,32]{1,2,0:T(8,128)(2,1)}, bf16[8,256,32]{1,2,0:T(8,128)(2,1)S(1)}, u32[]{:S(2)}) copy-start(bf16[8,256,32]{1,2,0:T(8,128)(2,1)S(1)} %all-to-all-done.2) | copy-start | bytes 393220
  93.6 112.7 %all-to-all-start.3 = ((bf16[8,3,704,256]{3,2,1,0:T(8,128)(2,1)}), bf16[8,3,704,256]{3,2,1,0:T(8,128)(2,1)}, u32[]{:S(2)}, u32[]{:S(2)}) async-start(bf16[8,3,704,256]{3,2,1,0:T(8,128)(2,1)} %stack.27), calls=%async_computation.3 | async-start | bytes 17301504 | tf_op jit(solution)/shard_map/all_to_all | solution.py:76
  109.6 55.8 %all-gather.7.cloned.1.call-start = ((), (), s32[]{:S(2)}) async-start(), calls=%async_computation.5 | async-start | bytes 1179648 | tf_op jit(solution)/shard_map/all_gather | solution.py:69
  212.7 1.2 copy-start
  222.2 8.3 %copy-start.6 = (f32[512,2]{0,1:T(2,128)S(1)}, f32[512,2]{0,1:T(2,128)}, u32[]{:S(2)}) copy-start(f32[512,2]{0,1:T(2,128)} %param.12) | copy-start | bytes 12292
  222.2 8.7 %copy-start.7 = (s32[512]{0:T(512)S(1)}, s32[512]{0:T(512)}, u32[]{:S(2)}) copy-start(s32[512]{0:T(512)} %param.17) | copy-start | bytes 6148
  224.5 56.3 %all-to-all-start.4 = ((bf16[256,64,32]{0,2,1:T(8,128)(2,1)}), bf16[256,64,32]{0,2,1:T(8,128)(2,1)S(1)}, u32[]{:S(2)}, u32[]{:S(2)}) async-start(bf16[256,64,32]{0,2,1:T(8,128)(2,1)} %bitcast.15), calls=%async_computation.4 | async-start | bytes 2097152 | tf_op jit(solution)/shard_map/all_to_all | solution.py:82
  281.3 36.8 %copy-start.8 = (f32[32]{0:T(128)S(1)}, f32[32]{0:T(128)}, u32[]{:S(2)}) copy-start(f32[32]{0:T(128)} %param.16) | copy-start | bytes 388
Sparse Core Ops, SparseCore 0:
  112.5 52.8 all-gather.6
